TPU v7x, 256 devices: a whole 4x4x8 slice. The times are simulated.
256 devices in a mesh: seq: 8 (over z), exp: 8 (over x, y_hi), img: 4 (over y_lo, core).
Axes of the slice: x: 4, y: 4 (y_hi: 2, y_lo: 2; y = y_hi * 2 + y_lo), z: 8, core: 2. Of those that a mesh axis runs over, the one named last changes fastest.
Arguments:
- projected: bfloat16 [32, 1024, 3, 1280], P(('img', 'exp'), 'seq'), parts along dimension 0, may hold values from -6 to 6
- residual: bfloat16 [32, 1024, 1280], P(('img', 'exp'), 'seq'), parts along dimension 0, may hold values from -6 to 6
- attn_proj: bfloat16 [1280, 1280], P('seq'), may hold values from -0.15625 to 0.15625
- norm_gain: float32 [1280], replicated, may hold values from 0.5 to 2
- norm_bias: float32 [1280], replicated, may hold values from -3 to 3
- expert_ids: int32 [32, 1024, 1], P(('img', 'exp')), parts along dimension 0, may hold values from 0 to 15; in each aligned block of 128 rows (0 to 127, 128 to 255, ..., all dimensions but the last counted through in order) at most 12 rows name the same one
- expert_up: bfloat16 [16, 1280, 5120], P('exp', None, 'seq'), may hold values from -0.15625 to 0.15625
- expert_down: bfloat16 [16, 5120, 1280], P('exp', 'seq'), may hold values from -0.078125 to 0.078125
Outputs:
- layer_out: bfloat16 [32, 1024, 1280], P(('img', 'exp'), 'seq'), parts along dimension 0
There are 4 independent parts, one for each index of `img`. A program takes and returns all parts, laid end to end along the dimension named above; an argument that names none is the same for every part. Nothing has to cross between parts.
Inputs may be any that keep to these rules, and one draw needn't show every extreme that they name: `expert_ids`: in each sequence, within every aligned block of 128 tokens, no expert is named by more than 12 tokens.
All inputs are finite; a program needn't handle non-finite values.
Results may differ from a plain program's by a relative error of at most 0.015.
Values may be sent and summed in bfloat16 or wider, within the bound.
No kernel may reach another device: no remote copies, remote signals or barrier semaphores. Data moves between devices by JAX's collectives and lax.ppermute only.
A program may use at most 64 MiB of HBM per device.

v0:
```python
import jax
import jax.numpy as jnp
from jax import lax
from jax.sharding import PartitionSpec as P

HEADS = 16
HEAD_DIM = 80


def attend(gathered):
    queries = gathered[:, 0, 0]
    keys_all = gathered[:, 1, 0]
    values = gathered[:, 2, 0]
    length = queries.shape[0]
    span_rows = min(512, length)
    factor = 1.0 / queries.shape[2] ** 0.5

    def one_block(offset):
        query_rows = lax.dynamic_slice_in_dim(queries, offset, span_rows, 0)
        scores = (
            jnp.einsum("qhd,khd->hqk", query_rows, keys_all, preferred_element_type=jnp.float32)
            * factor
        )
        peak = jnp.max(scores, axis=-1, keepdims=True)
        powers = jnp.exp(scores - peak)
        weights = (powers / jnp.sum(powers, axis=-1, keepdims=True)).astype(jnp.bfloat16)
        mixed = jnp.einsum("hqk,khd->qhd", weights, values, preferred_element_type=jnp.float32)
        return mixed.astype(jnp.bfloat16)

    starts = jnp.arange(length // span_rows, dtype=jnp.int32) * span_rows
    blocks = lax.map(one_block, starts)
    return blocks.reshape(length, queries.shape[1], queries.shape[2])


def layer_norm(stream, norm_gain, norm_bias):
    values = stream.astype(jnp.float32)
    centre = jnp.mean(values, axis=-1, keepdims=True)
    centered = values - centre
    variance = jnp.mean(centered * centered, axis=-1, keepdims=True)
    return (centered / jnp.sqrt(variance + 1e-06) * norm_gain + norm_bias).astype(jnp.bfloat16)


def per_device(
    projected, residual, attn_proj, norm_gain, norm_bias, expert_ids, expert_up, expert_down
):
    tok_rows = projected.shape[1]
    model_width = projected.shape[3]
    seq_count = lax.axis_size("seq")
    exp_count = lax.axis_size("exp")
    local_experts = expert_up.shape[0]
    experts = local_experts * exp_count
    cap_dev = 3 * tok_rows // (2 * experts)
    capacity = cap_dev * seq_count
    length = tok_rows * seq_count
    heads_here = HEADS // seq_count
    head_width = heads_here * HEAD_DIM
    regrouped = projected[0].reshape(tok_rows, 3, seq_count, heads_here, HEAD_DIM)
    attended = attend(lax.all_to_all(regrouped, "seq", split_axis=2, concat_axis=0, tiled=True))
    attended = attended.reshape(seq_count, tok_rows, 1, head_width)
    token_heads = lax.all_to_all(attended, "seq", split_axis=0, concat_axis=2, tiled=True).reshape(
        tok_rows, model_width
    )
    projected_sum = jnp.dot(
        token_heads,
        lax.all_gather(attn_proj, "seq", axis=0, tiled=True),
        preferred_element_type=jnp.float32,
    )
    stream_own = residual[0].astype(jnp.float32) + projected_sum
    stream = stream_own.astype(jnp.bfloat16)
    stream_own = stream.astype(jnp.float32)
    normed = layer_norm(stream, norm_gain, norm_bias)
    ids_flat = expert_ids[0, :, 0]
    onehot = (ids_flat[:, None] == jnp.arange(experts, dtype=jnp.int32)[None, :]).astype(jnp.int32)
    blocks = onehot.reshape(seq_count, tok_rows, experts)
    before = jnp.cumsum(blocks, axis=1) - blocks
    order_in_block = jnp.sum(before * blocks, axis=2).reshape(length)
    block_id = jnp.arange(length, dtype=jnp.int32) // tok_rows
    slot_all = ids_flat * capacity + block_id * cap_dev + order_in_block
    normed_all = lax.all_gather(normed, "seq", axis=0, tiled=True)
    buffer = jnp.zeros((experts * capacity, model_width), jnp.bfloat16).at[slot_all].set(normed_all)
    buffer = buffer.reshape(exp_count, local_experts, capacity, model_width)
    arrived = lax.all_to_all(buffer, "exp", split_axis=0, concat_axis=0, tiled=True)
    hidden = jax.nn.gelu(
        jnp.einsum("secd,edf->secf", arrived, expert_up, preferred_element_type=jnp.float32),
        approximate=False,
    ).astype(jnp.bfloat16)
    pieces = jnp.einsum(
        "secf,efd->secd", hidden, expert_down, preferred_element_type=jnp.float32
    ).astype(jnp.bfloat16)
    returned = lax.all_to_all(pieces, "exp", split_axis=0, concat_axis=0, tiled=True).reshape(
        experts * capacity, model_width
    )
    per_token = jnp.take(returned, slot_all, axis=0).astype(jnp.float32)
    expert_out = lax.psum_scatter(
        per_token.astype(jnp.bfloat16), "seq", scatter_dimension=0, tiled=True
    ).astype(jnp.float32)
    return (stream_own + expert_out).astype(jnp.bfloat16)[None]


def solution(mesh):
    return jax.shard_map(
        per_device,
        mesh=mesh,
        in_specs=(
            P(("img", "exp"), "seq", None, None),
            P(("img", "exp"), "seq", None),
            P("seq", None),
            P(),
            P(),
            P(("img", "exp"), None, None),
            P("exp", None, "seq"),
            P("exp", "seq", None),
        ),
        out_specs=P(("img", "exp"), "seq", None),
        check_vma=False,
    )
```

profile of v0, /device:TPU:8, one launch (start us, length us, event | category | flops | bytes accessed | tf_op | source)
XLA Modules:
  0.0 343.8 jit_solution(7028651593634963282)
XLA Ops:
  6.5 0.0 copy-start
  6.5 0.0 all-gather.3.cloned.1.call-start
  6.5 0.7 all-gather.3.cloned.1.call-update
  7.3 2.5 copy.32
  9.8 2.2 copy.33
  12.0 8.5 %all-to-all-start = ((bf16[128,3,8,2,80]{0,4,3,1,2:T(8,128)(2,1)}), bf16[128,3,8,2,80]{0,4,3,1,2:T(8,128)(2,1)}, u32[]{:S(2)}, u32[]{:S(2)}) async-start(bf16[128,3,8,2,80]{0,4,3,1,2:T(8,128)(2,1)} %copy.33), calls=%async_computation | async-start | bytes 1966080 | tf_op jit(solution)/shard_map/all_to_all | solution.py:58
  20.4 0.0 all-gather.5.cloned.1.call-start
  20.5 37.9 %all-to-all-done = bf16[128,3,8,2,80]{0,4,3,1,2:T(8,128)(2,1)} async-done(((bf16[128,3,8,2,80]{0,4,3,1,2:T(8,128)(2,1)}), bf16[128,3,8,2,80]{0,4,3,1,2:T(8,128)(2,1)}, u32[]{:S(2)}, u32[]{:S(2)}) %all-to-all-start) | async-done | bytes 983072 | tf_op jit(solution)/shard_map/all_to_all | solution.py:58
  58.4 1.3 copy_bitcast_fusion
  59.7 1.0 slice_bitcast_fusion
  60.7 22.1 %while.10 = (s32[]{:T(128)}, bf16[2,512,2,80]{1,3,2,0:T(8,128)(2,1)}, s32[2]{0:T(128)S(1)}, bf16[1024,2,80]{0,2,1:T(8,128)(2,1)}, bf16[1024,2,80]{0,2,1:T(8,128)...) while((s32[]{:T(128)}, bf16[2,512,2,80]{1,3,2,0:T(8,128)(2,1)}, ...), condition=%wide.region_3.4_spmd, body=%wide.region_0.3_spmd.sunk | while | flops 340870144 | bytes 9380495 | solution.py:31
  60.7 0.7 dynamic_slice.22
  63.5 4.6 %fusion.154 = (f32[2,512]{1,0:T(2,128)S(1)}, f32[2,512,1024]{2,1,0:T(8,128)}) fusion(bf16[1024,2,80]{0,2,1:T(8,128)(2,1)} %get-tuple-element.120, bf16[1024,2,80]{0,2,1:T(8,128)(2,1)} %get-tuple-element.119, s32[]{:T(128)S(6)} %select_n.70), kind=kOutput, calls=%fused_computation.154.clone.1 | convolution fusion | flops 170918912 | bytes 4689924 | tf_op jit(solution)/shard_map/while/body/eval_jaxpr/sub | solution.py:25
  68.0 3.8 %fusion.155 = bf16[2,512,2,80]{1,3,2,0:T(8,128)(2,1)} fusion(bf16[2,512,2,80]{1,3,2,0:T(8,128)(2,1)} %get-tuple-element.108, s32[]{:T(128)} %get-tuple-element.107, bf16[1024,2,80]{0,2,1:T(8,128)(2,1)} %get-tuple-element.121, f32[2,512,1024]{2,1,0:T(8,128)} %get-tuple-element.96, f32[2,512]{1,0:T(2,128)S(1)} %get-tuple-element.97), kind=kOutput, calls=%fused_computation.11.clone.1 | convolution fusion | flops 169951232 | bytes 4690432 | tf_op jit(solution)/shard_map/while/body/eval_jaxpr/hqk,khd->qhd/dot_general | solution.py:27
  71.8 0.7 dynamic_slice.22
  74.6 4.5 %fusion.154 = (f32[2,512]{1,0:T(2,128)S(1)}, f32[2,512,1024]{2,1,0:T(8,128)}) fusion(bf16[1024,2,80]{0,2,1:T(8,128)(2,1)} %get-tuple-element.120, bf16[1024,2,80]{0,2,1:T(8,128)(2,1)} %get-tuple-element.119, s32[]{:T(128)S(6)} %select_n.70), kind=kOutput, calls=%fused_computation.154.clone.1 | convolution fusion | flops 170918912 | bytes 4689924 | tf_op jit(solution)/shard_map/while/body/eval_jaxpr/sub | solution.py:25
  79.1 3.7 %fusion.155 = bf16[2,512,2,80]{1,3,2,0:T(8,128)(2,1)} fusion(bf16[2,512,2,80]{1,3,2,0:T(8,128)(2,1)} %get-tuple-element.108, s32[]{:T(128)} %get-tuple-element.107, bf16[1024,2,80]{0,2,1:T(8,128)(2,1)} %get-tuple-element.121, f32[2,512,1024]{2,1,0:T(8,128)} %get-tuple-element.96, f32[2,512]{1,0:T(2,128)S(1)} %get-tuple-element.97), kind=kOutput, calls=%fused_computation.11.clone.1 | convolution fusion | flops 169951232 | bytes 4690432 | tf_op jit(solution)/shard_map/while/body/eval_jaxpr/hqk,khd->qhd/dot_general | solution.py:27
  82.8 0.0 copy-start.3
  82.8 0.0 copy-start.4
  82.8 2.0 copy.35
  84.9 1.9 reshape_reshape.3
  86.8 1.0 copy.36
  87.8 16.6 %all_to_all.43 = bf16[8,128,1,160]{1,3,2,0:T(8,128)(2,1)} all-to-all(bf16[8,128,1,160]{1,3,2,0:T(8,128)(2,1)S(1)} %copy.36), channel_id=1, replica_groups=mesh['seq'=8,'exp'=8,'img'=4] {'seq'}, dimensions={0} | all-to-all | bytes 655360 | tf_op jit(solution)/shard_map/all_to_all | solution.py:60
  104.4 2.8 fusion.139
  107.2 0.0 copy-start.1
  107.2 0.2 multiply_reduce_fusion.1
  107.4 0.6 copy-done.1
  108.1 0.0 copy-done.3
  108.1 0.0 copy-done.4
  108.1 0.9 add_convert_fusion.1
  109.0 0.0 all-gather.5.cloned.1.call-update
  109.0 0.0 copy-done.2
  109.0 0.1 copy.37
  109.1 2.5 select_reduce_fusion
  111.7 35.8 %all-gather.5.cloned.1.call-done = bf16[1024,1280]{1,0:T(8,128)(2,1)} async-done(((bf16[128,1280]{1,0:T(8,128)(2,1)}), bf16[1024,1280]{1,0:T(8,128)(2,1)}) %all-gather.5.cloned.1.call-update) | async-done | bytes 2621456 | tf_op jit(solution)/shard_map/all_gather | solution.py:79
  147.5 8.6 %scatter_custom_fusion = bf16[1536,1280]{1,0:T(8,128)(2,1)} fusion(s32[1024]{0:T(1024)S(1)} %bitcast.147, bf16[1024,1280]{1,0:T(8,128)(2,1)} %all-gather.5.cloned.1.call-done, bf16[]{:T(256)} %constant.31.clone.1), kind=kCustom, calls=%fused_computation.83 | custom fusion | bytes 3932672 | tf_op jit(solution)/shard_map/scatter | solution.py:80
  156.1 50.5 %all_to_all.44 = bf16[8,2,96,1280]{3,2,1,0:T(8,128)(2,1)} all-to-all(bf16[8,2,96,1280]{3,2,1,0:T(8,128)(2,1)} %bitcast.142), channel_id=1, replica_groups=mesh['seq'=8,'exp'=8,'img'=4] {'exp'}, dimensions={0} | all-to-all | bytes 7864320 | tf_op jit(solution)/shard_map/all_to_all | solution.py:82
  206.6 0.0 copy-done
  206.6 17.1 %fusion.43 = bf16[8,2,96,1280]{3,2,0,1:T(8,128)(2,1)} fusion(bf16[2,640,1280]{2,1,0:T(8,128)(2,1)S(1)} %copy-done, bf16[8,2,96,1280]{3,2,1,0:T(8,128)(2,1)} %all_to_all.44, bf16[2,1280,640]{2,1,0:T(8,128)(2,1)} %param.16), kind=kOutput, calls=%fused_computation.46 | convolution fusion | flops 5099028480 | bytes 14417920 | tf_op jit(solution)/shard_map/secf,efd->secd/dot_general | solution.py:87
  223.7 4.3 %copy.41 = bf16[8,2,96,1280]{3,2,1,0:T(8,128)(2,1)} copy(bf16[8,2,96,1280]{3,2,0,1:T(8,128)(2,1)} %fusion.43) | data formatting | bytes 7864320 | tf_op jit(solution)/shard_map/convert_element_type | solution.py:89
  228.0 4.5 %all-to-all-start.3 = ((bf16[8,2,96,1280]{3,2,1,0:T(8,128)(2,1)}), bf16[8,2,96,1280]{3,2,1,0:T(8,128)(2,1)}, u32[]{:S(2)}, u32[]{:S(2)}) async-start(bf16[8,2,96,1280]{3,2,1,0:T(8,128)(2,1)} %copy.41), calls=%async_computation.3 | async-start | bytes 7864320 | tf_op jit(solution)/shard_map/all_to_all | solution.py:90
  232.5 0.0 reduce-scatter.2.cloned.1.call-start
  232.6 50.5 %all-to-all-done.3 = bf16[8,2,96,1280]{3,2,1,0:T(8,128)(2,1)} async-done(((bf16[8,2,96,1280]{3,2,1,0:T(8,128)(2,1)}), bf16[8,2,96,1280]{3,2,1,0:T(8,128)(2,1)}, u32[]{:S(2)}, u32[]{:S(2)}) %all-to-all-start.3) | async-done | bytes 3932192 | tf_op jit(solution)/shard_map/all_to_all | solution.py:90
  283.1 9.2 %gather_fusion = bf16[1024,1280]{1,0:T(8,128)(2,1)} fusion(bf16[1536,1280]{1,0:T(8,128)(2,1)} %bitcast.27, s32[1024]{0:T(1024)S(1)} %broadcast_clamp_fusion), kind=kCustom, calls=%fused_computation | custom fusion | bytes 5246976 | tf_op jit(solution)/shard_map/jit(_take)/gather | solution.py:93
  292.3 3.5 %broadcast_select_fusion = bf16[1024,1280]{1,0:T(8,128)(2,1)} fusion(bf16[1024,1280]{1,0:T(8,128)(2,1)} %gather_fusion, pred[1024]{0:T(1024)(128)(4,1)S(1)} %compare_and_fusion), kind=kLoop, calls=%fused_computation.49 | loop fusion | flops 1310720 | bytes 5243904 | tf_op jit(solution)/shard_map/jit(_take)/select_n | solution.py:93
  295.9 0.0 reduce-scatter.2.cloned.1.call-update
  295.9 39.4 %reduce-scatter.2.cloned.1.call-done = bf16[128,1280]{1,0:T(8,128)(2,1)} async-done(((bf16[1024,1280]{1,0:T(8,128)(2,1)}), bf16[128,1280]{1,0:T(8,128)(2,1)}) %reduce-scatter.2.cloned.1.call-update) | async-done | bytes 327696 | tf_op jit(solution)/shard_map/reduce_scatter | solution.py:94
  335.3 1.9 fusion.93
  (11 shorter events, 0.1 us)
Async XLA Ops:
  6.5 200.1 %copy-start = (bf16[2,640,1280]{2,1,0:T(8,128)(2,1)S(1)}, bf16[2,640,1280]{2,1,0:T(8,128)(2,1)}, u32[]{:S(2)}) copy-start(bf16[2,640,1280]{2,1,0:T(8,128)(2,1)} %param.17) | copy-start | bytes 9830404
  6.5 97.9 %all-gather.3.cloned.1.call-start = ((), (), s32[]{:S(2)}) async-start(), calls=%async_computation.5 | async-start | bytes 3686400 | tf_op jit(solution)/shard_map/all_gather | solution.py:65
  12.0 46.4 %all-to-all-start = ((bf16[128,3,8,2,80]{0,4,3,1,2:T(8,128)(2,1)}), bf16[128,3,8,2,80]{0,4,3,1,2:T(8,128)(2,1)}, u32[]{:S(2)}, u32[]{:S(2)}) async-start(bf16[128,3,8,2,80]{0,4,3,1,2:T(8,128)(2,1)} %copy.33), calls=%async_computation | async-start | bytes 1966080 | tf_op jit(solution)/shard_map/all_to_all | solution.py:58
  20.4 127.1 %all-gather.5.cloned.1.call-start = ((), (), s32[]{:S(2)}) async-start(), calls=%async_computation.6 | async-start | bytes 2949120 | tf_op jit(solution)/shard_map/all_gather | solution.py:79
  82.8 25.2 %copy-start.3 = (f32[1280]{0:T(1024)S(1)}, f32[1280]{0:T(1024)}, u32[]{:S(2)}) copy-start(f32[1280]{0:T(1024)} %param.14) | copy-start | bytes 15364
  82.8 25.3 %copy-start.4 = (f32[1280]{0:T(1024)S(1)}, f32[1280]{0:T(1024)}, u32[]{:S(2)}) copy-start(f32[1280]{0:T(1024)} %param.13) | copy-start | bytes 15364
  86.8 22.2 %copy-start.2 = (s32[1,1024,1]{1,2,0:T(1,128)S(1)}, s32[1,1024,1]{1,2,0:T(1,128)}, u32[]{:S(2)}) copy-start(s32[1,1024,1]{1,2,0:T(1,128)} %param.15) | copy-start | bytes 12292
  107.2 0.9 copy-start.1
  228.0 55.1 %all-to-all-start.3 = ((bf16[8,2,96,1280]{3,2,1,0:T(8,128)(2,1)}), bf16[8,2,96,1280]{3,2,1,0:T(8,128)(2,1)}, u32[]{:S(2)}, u32[]{:S(2)}) async-start(bf16[8,2,96,1280]{3,2,1,0:T(8,128)(2,1)} %copy.41), calls=%async_computation.3 | async-start | bytes 7864320 | tf_op jit(solution)/shard_map/all_to_all | solution.py:90
  232.5 102.8 %reduce-scatter.2.cloned.1.call-start = ((), (), s32[]{:S(2)}) async-start(), calls=%async_computation.7 | async-start | bytes 2949120 | tf_op jit(solution)/shard_map/reduce_scatter | solution.py:94
Sparse Core Ops, SparseCore 0:
  9.1 67.2 all-gather.2
  109.1 38.3 all-gather.4
  296.0 39.2 reduce-scatter.1
where the time goes:
time: 344 us
  waiting for transfers between devices  164 us (48%)
  blocking collectives  67.1 us (20%)
  matrix products  36.5 us (11%)
  local copies, waits for them, and re-layouts  36.3 us (11%)
  between operations  13.2 us (4%)
  starting transfers between devices  13.1 us (4%)
  other arithmetic  9.21 us (3%)
  loops' own time  4.15 us (1%)
    all_to_all x1, blocking collectives, per_device(): lax.all_to_all(buffer, 'exp', split_axis=0, concat_axis=0, tiled=True)  50.5 us
    all_to_all x1, waiting for transfers between devices, per_device(): lax.all_to_all(pieces, 'exp', split_axis=0, concat_axis=0, tiled=True)  50.5 us
    reduce_scatter x1, waiting for transfers between devices, per_device(): lax.psum_scatter(per_token.astype(jnp.bfloat16), 'seq', scatter_dimension...  39.4 us
    all_to_all x1, waiting for transfers between devices, per_device(): lax.all_to_all(regrouped, 'seq', split_axis=2, concat_axis=0, tiled=True)  37.9 us
    all_gather x1, waiting for transfers between devices, per_device(): normed_all = lax.all_gather(normed, 'seq', axis=0, tiled=True)  35.8 us
    dot_general x1, matrix products, per_device(): jnp.einsum('secf,efd->secd', hidden, expert_down, preferred_element_type=...  17.1 us
    all_to_all x1, blocking collectives, per_device(): lax.all_to_all(attended, 'seq', split_axis=0, concat_axis=2, tiled=True)  16.6 us
    gather x1, local copies, waits for them, and re-layouts, per_device(): per_token = jnp.take(returned, slot_all, axis=0).astype(jnp.float32)  9.22 us
  transfers between devices with their start and end apart: 5, of which 4 were waited for; matrix products, arithmetic and copies ran while one was open for 10% of the time, Pallas kernels for 0%

commit v1 on v0

--- a/solution.py
+++ b/solution.py
@@ -69,31 +69,33 @@
     stream = stream_own.astype(jnp.bfloat16)
     stream_own = stream.astype(jnp.float32)
     normed = layer_norm(stream, norm_gain, norm_bias)
-    ids_flat = expert_ids[0, :, 0]
-    onehot = (ids_flat[:, None] == jnp.arange(experts, dtype=jnp.int32)[None, :]).astype(jnp.int32)
-    blocks = onehot.reshape(seq_count, tok_rows, experts)
-    before = jnp.cumsum(blocks, axis=1) - blocks
-    order_in_block = jnp.sum(before * blocks, axis=2).reshape(length)
-    block_id = jnp.arange(length, dtype=jnp.int32) // tok_rows
-    slot_all = ids_flat * capacity + block_id * cap_dev + order_in_block
-    normed_all = lax.all_gather(normed, "seq", axis=0, tiled=True)
-    buffer = jnp.zeros((experts * capacity, model_width), jnp.bfloat16).at[slot_all].set(normed_all)
-    buffer = buffer.reshape(exp_count, local_experts, capacity, model_width)
-    arrived = lax.all_to_all(buffer, "exp", split_axis=0, concat_axis=0, tiled=True)
+    seq_index = lax.axis_index("seq")
+    ids_own = lax.dynamic_slice_in_dim(expert_ids[0, :, 0], seq_index * tok_rows, tok_rows)
+    onehot = (ids_own[:, None] == jnp.arange(experts, dtype=jnp.int32)[None, :]).astype(jnp.int32)
+    before = jnp.cumsum(onehot, axis=0) - onehot
+    order_in_block = jnp.sum(before * onehot, axis=1)
+    dest = ids_own * cap_dev + order_in_block
+    select = (dest[:, None] == jnp.arange(experts * cap_dev, dtype=jnp.int32)[None, :]).astype(
+        jnp.bfloat16
+    )
+    dispatch = jnp.einsum(
+        "tk,td->kd", select, normed, preferred_element_type=jnp.float32
+    ).astype(jnp.bfloat16)
+    dispatch = dispatch.reshape(exp_count, local_experts, cap_dev, model_width)
+    arrived = lax.all_to_all(dispatch, "exp", split_axis=0, concat_axis=0, tiled=True)
+    gathered = lax.all_gather(arrived, "seq", axis=0, tiled=False)
     hidden = jax.nn.gelu(
-        jnp.einsum("secd,edf->secf", arrived, expert_up, preferred_element_type=jnp.float32),
+        jnp.einsum("sejcd,jdf->sejcf", gathered, expert_up, preferred_element_type=jnp.float32),
         approximate=False,
     ).astype(jnp.bfloat16)
     pieces = jnp.einsum(
-        "secf,efd->secd", hidden, expert_down, preferred_element_type=jnp.float32
+        "sejcf,jfd->sejcd", hidden, expert_down, preferred_element_type=jnp.float32
     ).astype(jnp.bfloat16)
-    returned = lax.all_to_all(pieces, "exp", split_axis=0, concat_axis=0, tiled=True).reshape(
-        experts * capacity, model_width
+    summed = lax.psum_scatter(pieces, "seq", scatter_dimension=0, tiled=True)[0]
+    returned = lax.all_to_all(summed, "exp", split_axis=0, concat_axis=0, tiled=True).reshape(
+        experts * cap_dev, model_width
     )
-    per_token = jnp.take(returned, slot_all, axis=0).astype(jnp.float32)
-    expert_out = lax.psum_scatter(
-        per_token.astype(jnp.bfloat16), "seq", scatter_dimension=0, tiled=True
-    ).astype(jnp.float32)
+    expert_out = jnp.einsum("tk,kd->td", select, returned, preferred_element_type=jnp.float32)
     return (stream_own + expert_out).astype(jnp.bfloat16)[None]
 
 

time: 344 us -> 291 us (0.85)
  blocking collectives: 67.1 us -> 32.9 us
  waiting for transfers between devices: 164 us -> 147 us
  matrix products: 36.5 us -> 45 us
  other arithmetic: 9.21 us -> 1.32 us
    all_to_all x1, waiting for transfers between devices: 50.5 us -> 11.7 us  [per_device(): lax.all_to_all(attended, 'seq', split_axis=0, concat_axis=2, tiled=True)]
    all_to_all x2, blocking collectives: 67.1 us -> 32.9 us  [the longest x1 16.5 us: per_device(): lax.all_to_all(summed, 'exp', split_axis=0, concat_axis=0, tiled=True)]
    reduce_scatter x1, waiting for transfers between devices: 39.4 us -> 51.6 us  [per_device(): summed = lax.psum_scatter(pieces, 'seq', scatter_dimension=0, tiled=True)[0]]
    all_gather x1, waiting for transfers between devices: 35.8 us -> 45.5 us  [per_device(): gathered = lax.all_gather(arrived, 'seq', axis=0, tiled=False)]
    gather x1 -> x0, local copies, waits for them, and re-layouts: 9.22 us -> none  [per_device(): per_token = jnp.take(returned, slot_all, axis=0).astype(jnp.float32)]
    scatter x1 -> x0, local copies, waits for them, and re-layouts: 8.6 us -> none  [per_device(): jnp.zeros((experts * capacity, model_width), jnp.bfloat16).at[slot_all]]
    dot_general x1 -> x3, matrix products: 17.1 us -> 25.6 us  [the longest x1 22.1 us: per_device(): jnp.einsum('sejcf,jfd->sejcd', hidden, expert_down, preferred_element_typ...]
    reshape x0 -> x3, local copies, waits for them, and re-layouts: none -> 5.44 us  [the longest x2 3.45 us: per_device(): dispatch = dispatch.reshape(exp_count, local_experts, cap_dev, model_width)]
  transfers between devices with their start and end apart: 5 -> 5, of which waited for: 4 -> 4; matrix products, arithmetic and copies ran while one was open for 10% -> 11% of each run, Pallas kernels for 0% -> 0%
where the time goes in v1:
time: 291 us; the launch traced here: 290 us
  waiting for transfers between devices  147 us (51%)
  matrix products  45 us (15%)
  local copies, waits for them, and re-layouts  34.1 us (12%)
  blocking collectives  32.9 us (11%)
  between operations  13.2 us (5%)
  starting transfers between devices  12.8 us (4%)
  loops' own time  3.37 us (1%)
    reduce_scatter x1, waiting for transfers between devices, per_device(): summed = lax.psum_scatter(pieces, 'seq', scatter_dimension=0, tiled=True)[0]  51.6 us
    all_gather x1, waiting for transfers between devices, per_device(): gathered = lax.all_gather(arrived, 'seq', axis=0, tiled=False)  45.5 us
    all_to_all x1, waiting for transfers between devices, per_device(): lax.all_to_all(regrouped, 'seq', split_axis=2, concat_axis=0, tiled=True)  37.9 us
    dot_general x1, matrix products, per_device(): jnp.einsum('sejcf,jfd->sejcd', hidden, expert_down, preferred_element_typ...  22.1 us
    all_to_all x1, blocking collectives, per_device(): lax.all_to_all(summed, 'exp', split_axis=0, concat_axis=0, tiled=True)  16.5 us
    all_to_all x1, blocking collectives, per_device(): lax.all_to_all(dispatch, 'exp', split_axis=0, concat_axis=0, tiled=True)  16.4 us
    all_to_all x1, waiting for transfers between devices, per_device(): lax.all_to_all(attended, 'seq', split_axis=0, concat_axis=2, tiled=True)  11.7 us
    sub x2, matrix products, one_block(): powers = jnp.exp(scores - peak)  9.1 us
  transfers between devices with their start and end apart: 5, of which 4 were waited for; matrix products, arithmetic and copies ran while one was open for 11% of the time, Pallas kernels for 0%

profile of v1, /device:TPU:8, one launch (start us, length us, event | category | flops | bytes accessed | tf_op | source)
XLA Modules:
  0.0 290.2 jit_solution(802033393720290707)
XLA Ops:
  6.5 0.0 copy-start
  6.5 0.0 all-gather.4.cloned.1.call-start
  6.5 0.7 all-gather.4.cloned.1.call-update
  7.3 2.5 copy.22
  9.7 2.2 copy.23
  12.0 8.5 %all-to-all-start = ((bf16[128,3,8,2,80]{0,4,3,1,2:T(8,128)(2,1)}), bf16[128,3,8,2,80]{0,4,3,1,2:T(8,128)(2,1)}, u32[]{:S(2)}, u32[]{:S(2)}) async-start(bf16[128,3,8,2,80]{0,4,3,1,2:T(8,128)(2,1)} %copy.23), calls=%async_computation | async-start | bytes 1966080 | tf_op jit(solution)/shard_map/all_to_all | solution.py:58
  20.4 37.9 %all-to-all-done = bf16[128,3,8,2,80]{0,4,3,1,2:T(8,128)(2,1)} async-done(((bf16[128,3,8,2,80]{0,4,3,1,2:T(8,128)(2,1)}), bf16[128,3,8,2,80]{0,4,3,1,2:T(8,128)(2,1)}, u32[]{:S(2)}, u32[]{:S(2)}) %all-to-all-start) | async-done | bytes 983072 | tf_op jit(solution)/shard_map/all_to_all | solution.py:58
  58.4 1.3 copy_bitcast_fusion
  59.7 1.0 slice_bitcast_fusion
  60.7 21.2 %while.10 = (s32[]{:T(128)}, bf16[2,512,2,80]{1,3,2,0:T(8,128)(2,1)}, s32[2]{0:T(128)S(1)}, bf16[1024,2,80]{0,2,1:T(8,128)(2,1)}, bf16[1024,2,80]{0,2,1:T(8,128)...) while((s32[]{:T(128)}, bf16[2,512,2,80]{1,3,2,0:T(8,128)(2,1)}, ...), condition=%wide.region_3.4_spmd, body=%wide.region_0.3_spmd.sunk | while | flops 340870144 | bytes 9379995 | solution.py:31
  60.7 0.6 dynamic_slice.32
  63.0 4.6 %fusion.121 = (f32[2,512]{1,0:T(2,128)S(1)}, f32[2,512,1024]{2,1,0:T(8,128)}) fusion(bf16[1024,2,80]{0,2,1:T(8,128)(2,1)} %get-tuple-element.120, bf16[1024,2,80]{0,2,1:T(8,128)(2,1)} %get-tuple-element.119, s32[]{:T(128)S(6)} %select_n.8), kind=kOutput, calls=%fused_computation.115.clone.1 | convolution fusion | flops 170918912 | bytes 4689924 | tf_op jit(solution)/shard_map/while/body/eval_jaxpr/sub | solution.py:25
  67.5 3.8 %fusion.122 = bf16[2,512,2,80]{1,3,2,0:T(8,128)(2,1)} fusion(bf16[2,512,2,80]{1,3,2,0:T(8,128)(2,1)} %get-tuple-element.108, s32[]{:T(128)S(6)} %copy.39, bf16[1024,2,80]{0,2,1:T(8,128)(2,1)} %get-tuple-element.121, f32[2,512,1024]{2,1,0:T(8,128)} %get-tuple-element.96, f32[2,512]{1,0:T(2,128)S(1)} %get-tuple-element.97), kind=kOutput, calls=%fused_computation.9.clone.1 | convolution fusion | flops 169951232 | bytes 4689924 | tf_op jit(solution)/shard_map/while/body/eval_jaxpr/hqk,khd->qhd/dot_general | solution.py:27
  71.3 0.6 dynamic_slice.32
  73.6 4.5 %fusion.121 = (f32[2,512]{1,0:T(2,128)S(1)}, f32[2,512,1024]{2,1,0:T(8,128)}) fusion(bf16[1024,2,80]{0,2,1:T(8,128)(2,1)} %get-tuple-element.120, bf16[1024,2,80]{0,2,1:T(8,128)(2,1)} %get-tuple-element.119, s32[]{:T(128)S(6)} %select_n.8), kind=kOutput, calls=%fused_computation.115.clone.1 | convolution fusion | flops 170918912 | bytes 4689924 | tf_op jit(solution)/shard_map/while/body/eval_jaxpr/sub | solution.py:25
  78.1 3.7 %fusion.122 = bf16[2,512,2,80]{1,3,2,0:T(8,128)(2,1)} fusion(bf16[2,512,2,80]{1,3,2,0:T(8,128)(2,1)} %get-tuple-element.108, s32[]{:T(128)S(6)} %copy.39, bf16[1024,2,80]{0,2,1:T(8,128)(2,1)} %get-tuple-element.121, f32[2,512,1024]{2,1,0:T(8,128)} %get-tuple-element.96, f32[2,512]{1,0:T(2,128)S(1)} %get-tuple-element.97), kind=kOutput, calls=%fused_computation.9.clone.1 | convolution fusion | flops 169951232 | bytes 4689924 | tf_op jit(solution)/shard_map/while/body/eval_jaxpr/hqk,khd->qhd/dot_general | solution.py:27
  81.9 2.0 copy.25
  83.9 1.9 reshape_reshape.3
  85.8 1.7 copy.26
  87.6 4.1 %all-to-all-start.1 = ((bf16[8,128,1,160]{1,3,2,0:T(8,128)(2,1)}), bf16[8,128,1,160]{1,3,2,0:T(8,128)(2,1)}, u32[]{:S(2)}, u32[]{:S(2)}) async-start(bf16[8,128,1,160]{1,3,2,0:T(8,128)(2,1)} %copy.26), calls=%async_computation.1 | async-start | bytes 655360 | tf_op jit(solution)/shard_map/all_to_all | solution.py:60
  91.7 0.0 all-gather.6.cloned.1.call-start
  91.7 0.7 dynamic-slice_bitcast_fusion
  92.4 0.1 fusion.68
  92.5 0.2 reduce_window_sum.11
  92.6 0.2 select_reduce_fusion
  92.8 0.7 multiply_add_fusion
  93.5 11.7 %all-to-all-done.1 = bf16[8,128,1,160]{1,3,2,0:T(8,128)(2,1)} async-done(((bf16[8,128,1,160]{1,3,2,0:T(8,128)(2,1)}), bf16[8,128,1,160]{1,3,2,0:T(8,128)(2,1)}, u32[]{:S(2)}, u32[]{:S(2)}) %all-to-all-start.1) | async-done | bytes 327712 | tf_op jit(solution)/shard_map/all_to_all | solution.py:60
  105.2 2.8 fusion.104
  108.0 0.0 copy-start.1
  108.0 0.2 multiply_reduce_fusion.1
  108.2 0.6 copy-done.1
  108.9 1.2 convolution_convert_fusion.1
  110.1 2.0 reshape.40
  112.0 1.5 copy.27
  113.5 16.4 %all_to_all.43 = bf16[8,2,12,1280]{3,1,2,0:T(2,128)(2,1)} all-to-all(bf16[8,2,12,1280]{3,1,2,0:T(2,128)(2,1)S(1)} %copy.27), channel_id=1, replica_groups=mesh['seq'=8,'exp'=8,'img'=4] {'exp'}, dimensions={0} | all-to-all | bytes 983040 | tf_op jit(solution)/shard_map/all_to_all | solution.py:85
  129.9 0.0 all-gather.6.cloned.1.call-update
  129.9 0.2 reduce-scatter.2.cloned.1.call-start
  130.2 45.5 %all-gather.6.cloned.1.call-done = bf16[64,2,12,1280]{3,1,2,0:T(2,128)(2,1)} async-done(((bf16[8,2,12,1280]{3,1,2,0:T(2,128)(2,1)}), bf16[64,2,12,1280]{3,1,2,0:T(2,128)(2,1)}) %all-gather.6.cloned.1.call-update) | async-done | bytes 3932176 | tf_op jit(solution)/shard_map/all_gather | solution.py:86
  175.7 5.2 %copy.28 = bf16[64,2,12,1280]{3,2,0,1:T(8,128)(2,1)} copy(bf16[64,2,12,1280]{3,1,2,0:T(2,128)(2,1)} %all-gather.6.cloned.1.call-done) | data formatting | bytes 7864320 | tf_op jit(solution)/shard_map/all_gather | solution.py:86
  180.8 22.1 %fusion.41 = bf16[8,8,2,12,1280]{4,3,1,0,2:T(8,128)(2,1)} fusion(bf16[2,640,1280]{2,1,0:T(8,128)(2,1)S(1)} %copy-done, bf16[8,8,2,12,1280]{4,3,1,0,2:T(8,128)(2,1)} %bitcast.136, bf16[2,1280,640]{2,1,0:T(8,128)(2,1)} %param.16), kind=kOutput, calls=%fused_computation.42 | convolution fusion | flops 5099028480 | bytes 14417920 | tf_op jit(solution)/shard_map/sejcf,jfd->sejcd/dot_general | solution.py:91
  202.9 5.9 %copy.29 = bf16[8,8,2,12,1280]{4,1,3,2,0:T(8,128)(2,1)} copy(bf16[8,8,2,12,1280]{4,3,1,0,2:T(8,128)(2,1)} %fusion.41) | data formatting | bytes 7864320 | tf_op jit(solution)/shard_map/convert_element_type | solution.py:93
  208.8 0.0 reduce-scatter.2.cloned.1.call-update
  208.8 51.6 %reduce-scatter.2.cloned.1.call-done = bf16[1,8,2,12,1280]{4,1,3,2,0:T(8,128)(2,1)} async-done(((bf16[8,8,2,12,1280]{4,1,3,2,0:T(8,128)(2,1)}), bf16[1,8,2,12,1280]{4,1,3,2,0:T(8,128)(2,1)}) %reduce-scatter.2.cloned.1.call-update) | async-done | bytes 491536 | tf_op jit(solution)/shard_map/reduce_scatter | solution.py:94
  260.4 1.5 copy.30
  262.0 16.5 %all_to_all.44 = bf16[8,2,12,1280]{3,1,2,0:T(2,128)(2,1)S(1)} all-to-all(bf16[8,2,12,1280]{3,1,2,0:T(2,128)(2,1)S(1)} %copy.30), channel_id=1, replica_groups=mesh['seq'=8,'exp'=8,'img'=4] {'exp'}, dimensions={0} | all-to-all | bytes 983040 | tf_op jit(solution)/shard_map/all_to_all | solution.py:95
  278.5 0.9 copy.31
  279.4 2.0 reshape.41
  281.4 2.3 fusion.65
  (10 shorter events, 0.0 us)
Async XLA Ops:
  6.5 174.3 %copy-start = (bf16[2,640,1280]{2,1,0:T(8,128)(2,1)S(1)}, bf16[2,640,1280]{2,1,0:T(8,128)(2,1)}, u32[]{:S(2)}) copy-start(bf16[2,640,1280]{2,1,0:T(8,128)(2,1)} %param.17) | copy-start | bytes 9830404
  6.5 98.7 %all-gather.4.cloned.1.call-start = ((), (), s32[]{:S(2)}) async-start(), calls=%async_computation.5 | async-start | bytes 3686400 | tf_op jit(solution)/shard_map/all_gather | solution.py:65
  12.0 46.4 %all-to-all-start = ((bf16[128,3,8,2,80]{0,4,3,1,2:T(8,128)(2,1)}), bf16[128,3,8,2,80]{0,4,3,1,2:T(8,128)(2,1)}, u32[]{:S(2)}, u32[]{:S(2)}) async-start(bf16[128,3,8,2,80]{0,4,3,1,2:T(8,128)(2,1)} %copy.23), calls=%async_computation | async-start | bytes 1966080 | tf_op jit(solution)/shard_map/all_to_all | solution.py:58
  81.9 27.0 %copy-start.2 = (f32[1280]{0:T(1024)S(1)}, f32[1280]{0:T(1024)}, u32[]{:S(2)}) copy-start(f32[1280]{0:T(1024)} %param.14) | copy-start | bytes 15364
  81.9 27.0 %copy-start.3 = (f32[1280]{0:T(1024)S(1)}, f32[1280]{0:T(1024)}, u32[]{:S(2)}) copy-start(f32[1280]{0:T(1024)} %param.13) | copy-start | bytes 15364
  87.6 17.6 %all-to-all-start.1 = ((bf16[8,128,1,160]{1,3,2,0:T(8,128)(2,1)}), bf16[8,128,1,160]{1,3,2,0:T(8,128)(2,1)}, u32[]{:S(2)}, u32[]{:S(2)}) async-start(bf16[8,128,1,160]{1,3,2,0:T(8,128)(2,1)} %copy.26), calls=%async_computation.1 | async-start | bytes 655360 | tf_op jit(solution)/shard_map/all_to_all | solution.py:60
  91.7 84.0 %all-gather.6.cloned.1.call-start = ((), (), s32[]{:S(2)}) async-start(), calls=%async_computation.7 | async-start | bytes 4423680 | tf_op jit(solution)/shard_map/all_gather | solution.py:86
  108.0 0.9 copy-start.1
  129.9 130.5 %reduce-scatter.2.cloned.1.call-start = ((), (), s32[]{:S(2)}) async-start(), calls=%async_computation.6 | async-start | bytes 4423680 | tf_op jit(solution)/shard_map/reduce_scatter | solution.py:94
Sparse Core Ops, SparseCore 0:
  9.1 67.2 all-gather.3
  130.1 45.5 all-gather.5
  209.0 51.4 reduce-scatter.1

commit v2 on v1

--- a/solution.py
+++ b/solution.py
@@ -74,29 +74,41 @@
     onehot = (ids_own[:, None] == jnp.arange(experts, dtype=jnp.int32)[None, :]).astype(jnp.int32)
     before = jnp.cumsum(onehot, axis=0) - onehot
     order_in_block = jnp.sum(before * onehot, axis=1)
-    dest = ids_own * cap_dev + order_in_block
-    select = (dest[:, None] == jnp.arange(experts * cap_dev, dtype=jnp.int32)[None, :]).astype(
-        jnp.bfloat16
-    )
-    dispatch = jnp.einsum(
-        "tk,td->kd", select, normed, preferred_element_type=jnp.float32
-    ).astype(jnp.bfloat16)
-    dispatch = dispatch.reshape(exp_count, local_experts, cap_dev, model_width)
-    arrived = lax.all_to_all(dispatch, "exp", split_axis=0, concat_axis=0, tiled=True)
-    gathered = lax.all_gather(arrived, "seq", axis=0, tiled=False)
-    hidden = jax.nn.gelu(
-        jnp.einsum("sejcd,jdf->sejcf", gathered, expert_up, preferred_element_type=jnp.float32),
-        approximate=False,
-    ).astype(jnp.bfloat16)
-    pieces = jnp.einsum(
-        "sejcf,jfd->sejcd", hidden, expert_down, preferred_element_type=jnp.float32
-    ).astype(jnp.bfloat16)
-    summed = lax.psum_scatter(pieces, "seq", scatter_dimension=0, tiled=True)[0]
-    returned = lax.all_to_all(summed, "exp", split_axis=0, concat_axis=0, tiled=True).reshape(
-        experts * cap_dev, model_width
-    )
-    expert_out = jnp.einsum("tk,kd->td", select, returned, preferred_element_type=jnp.float32)
-    return (stream_own + expert_out).astype(jnp.bfloat16)[None]
+    dest = (ids_own // local_experts) * cap_dev + order_in_block
+    columns = jnp.arange(exp_count * cap_dev, dtype=jnp.int32)[None, :]
+    expert_out = stream_own
+    for local in range(local_experts):
+        select = (
+            (dest[:, None] == columns) & (ids_own % local_experts == local)[:, None]
+        ).astype(jnp.bfloat16)
+        dispatch = jnp.einsum(
+            "tk,td->kd", select, normed, preferred_element_type=jnp.float32
+        ).astype(jnp.bfloat16)
+        arrived = lax.all_to_all(
+            dispatch.reshape(exp_count, cap_dev, model_width),
+            "exp",
+            split_axis=0,
+            concat_axis=0,
+            tiled=True,
+        )
+        gathered = lax.all_gather(arrived, "seq", axis=0, tiled=True).reshape(-1, model_width)
+        hidden = jax.nn.gelu(
+            jnp.dot(gathered, expert_up[local], preferred_element_type=jnp.float32),
+            approximate=False,
+        ).astype(jnp.bfloat16)
+        pieces = jnp.dot(hidden, expert_down[local], preferred_element_type=jnp.float32).astype(
+            jnp.bfloat16
+        )
+        summed = lax.psum_scatter(
+            pieces.reshape(-1, cap_dev, model_width), "seq", scatter_dimension=0, tiled=True
+        )
+        returned = lax.all_to_all(
+            summed, "exp", split_axis=0, concat_axis=0, tiled=True
+        ).reshape(exp_count * cap_dev, model_width)
+        expert_out = expert_out + jnp.einsum(
+            "tk,kd->td", select, returned, preferred_element_type=jnp.float32
+        )
+    return expert_out.astype(jnp.bfloat16)[None]
 
 
 def solution(mesh):

time: 291 us -> 300 us (1.031)
  waiting for transfers between devices: 147 us -> 173 us
  local copies, waits for them, and re-layouts: 34.1 us -> 20.7 us
  starting transfers between devices: 12.8 us -> 24 us
  matrix products: 45 us -> 36.5 us
  blocking collectives: 32.9 us -> 26.7 us
    reduce_scatter x1 -> x2, waiting for transfers between devices: 51.6 us -> 69.4 us  [per_device(): lax.psum_scatter(pieces.reshape(-1, cap_dev, model_width), 'seq', scatter...]
    all_to_all x0 -> x2, starting transfers between devices: none -> 11.5 us  [per_device(): lax.all_to_all(summed, 'exp', split_axis=0, concat_axis=0, tiled=True)]
    all_to_all x0 -> x2, waiting for transfers between devices: none -> 8.34 us  [per_device(): lax.all_to_all(summed, 'exp', split_axis=0, concat_axis=0, tiled=True)]
    all_to_all x2, blocking collectives: 32.9 us -> 26.7 us  [per_device(): lax.all_to_all(dispatch.reshape(exp_count, cap_dev, model_width), 'exp',...]
    convert_element_type x1 -> x0, local copies, waits for them, and re-layouts: 5.89 us -> none  [per_device(): pieces = jnp.einsum('sejcf,jfd->sejcd', hidden, expert_down, preferred_el...]
    dot_general x1 -> x2, matrix products: 22.1 us -> 18.8 us  [per_device(): jnp.dot(hidden, expert_down[local], preferred_element_type=jnp.float32)]
    reshape x3 -> x8, local copies, waits for them, and re-layouts: 5.44 us -> 8.54 us  [the longest x2 4.29 us: per_device(): pieces.reshape(-1, cap_dev, model_width)]
    all_gather x1 -> x2, waiting for transfers between devices: 45.5 us -> 45.3 us  [per_device(): lax.all_gather(arrived, 'seq', axis=0, tiled=True).reshape(-1, model_width)]
  transfers between devices with their start and end apart: 5 -> 9, of which waited for: 4 -> 7; matrix products, arithmetic and copies ran while one was open for 11% -> 18% of each run, Pallas kernels for 0% -> 0%
where the time goes in v2:
time: 300 us; the launch traced here: 299 us
  waiting for transfers between devices  173 us (58%)
  matrix products  36.5 us (12%)
  blocking collectives  26.7 us (9%)
  starting transfers between devices  24 us (8%)
  local copies, waits for them, and re-layouts  20.7 us (7%)
  between operations  13.3 us (4%)
  loops' own time  3.4 us (1%)
    reduce_scatter x2, waiting for transfers between devices, per_device(): lax.psum_scatter(pieces.reshape(-1, cap_dev, model_width), 'seq', scatter...  69.4 us
    all_gather x2, waiting for transfers between devices, per_device(): lax.all_gather(arrived, 'seq', axis=0, tiled=True).reshape(-1, model_width)  45.3 us
    all_to_all x1, waiting for transfers between devices, per_device(): lax.all_to_all(regrouped, 'seq', split_axis=2, concat_axis=0, tiled=True)  36 us
    all_to_all x2, blocking collectives, per_device(): lax.all_to_all(dispatch.reshape(exp_count, cap_dev, model_width), 'exp',...  26.7 us
    dot_general x2, matrix products, per_device(): jnp.dot(hidden, expert_down[local], preferred_element_type=jnp.float32)  18.8 us
    all_to_all x1, waiting for transfers between devices, per_device(): lax.all_to_all(attended, 'seq', split_axis=0, concat_axis=2, tiled=True)  12.9 us
    all_to_all x2, starting transfers between devices, per_device(): lax.all_to_all(summed, 'exp', split_axis=0, concat_axis=0, tiled=True)  11.5 us
    all_to_all x1, starting transfers between devices, per_device(): lax.all_to_all(regrouped, 'seq', split_axis=2, concat_axis=0, tiled=True)  8.47 us
  transfers between devices with their start and end apart: 9, of which 7 were waited for; matrix products, arithmetic and copies ran while one was open for 18% of the time, Pallas kernels for 0%

profile of v2, /device:TPU:8, one launch (start us, length us, event | category | flops | bytes accessed | tf_op | source)
XLA Modules:
  0.0 299.0 jit_solution(7632882221548638373)
XLA Ops:
  6.5 0.7 all-gather.4.cloned.1.call-update
  7.3 1.6 copy.17
  8.9 1.0 copy.18
  9.9 8.5 %all-to-all-start = ((bf16[128,3,8,2,80]{0,4,3,1,2:T(8,128)(2,1)}), bf16[128,3,8,2,80]{0,4,3,1,2:T(8,128)(2,1)S(1)}, u32[]{:S(2)}, u32[]{:S(2)}) async-start(bf16[128,3,8,2,80]{0,4,3,1,2:T(8,128)(2,1)} %copy.18), calls=%async_computation | async-start | bytes 1966080 | tf_op jit(solution)/shard_map/all_to_all | solution.py:58
  18.3 0.7 broadcast_compare_fusion.1
  19.0 36.0 %all-to-all-done = bf16[128,3,8,2,80]{0,4,3,1,2:T(8,128)(2,1)S(1)} async-done(((bf16[128,3,8,2,80]{0,4,3,1,2:T(8,128)(2,1)}), bf16[128,3,8,2,80]{0,4,3,1,2:T(8,128)(2,1)S(1)}, u32[]{:S(2)}, u32[]{:S(2)}) %all-to-all-start) | async-done | bytes 983072 | tf_op jit(solution)/shard_map/all_to_all | solution.py:58
  55.3 17.7 %while.10 = (s32[]{:T(128)}, bf16[2,512,2,80]{1,3,2,0:T(8,128)(2,1)S(1)}, s32[2]{0:T(128)S(1)}, bf16[1024,2,80]{0,2,1:T(8,128)(2,1)S(1)}, bf16[1024,2,80]{0,2,1:...) while((s32[]{:T(128)}, bf16[2,512,2,80]{1,3,2,0:T(8,128)(2,1)S(1)}, ...), condition=%wide.region_3.4_spmd, body=%wide.region_0.3_spmd.sunk | while | flops 340870144 | bytes 9379995 | solution.py:31
  55.3 0.6 dynamic_slice.31
  57.6 3.5 %fusion.166 = (f32[2,512]{1,0:T(2,128)S(1)}, f32[2,512,1024]{2,1,0:T(8,128)}) fusion(bf16[1024,2,80]{0,2,1:T(8,128)(2,1)S(1)} %get-tuple-element.123, bf16[1024,2,80]{0,2,1:T(8,128)(2,1)S(1)} %get-tuple-element.122, s32[]{:T(128)S(6)} %select_n.43), kind=kOutput, calls=%fused_computation.168.clone.1 | convolution fusion | flops 170918912 | bytes 4689924 | tf_op jit(solution)/shard_map/while/body/eval_jaxpr/sub | solution.py:25
  61.1 3.1 %fusion.167 = bf16[2,512,2,80]{1,3,2,0:T(8,128)(2,1)S(1)} fusion(bf16[2,512,2,80]{1,3,2,0:T(8,128)(2,1)S(1)} %get-tuple-element.111, s32[]{:T(128)S(6)} %copy.31, bf16[1024,2,80]{0,2,1:T(8,128)(2,1)S(1)} %get-tuple-element.124, f32[2,512,1024]{2,1,0:T(8,128)} %get-tuple-element.99, f32[2,512]{1,0:T(2,128)S(1)} %get-tuple-element.100), kind=kOutput, calls=%fused_computation.9.clone.1 | convolution fusion | flops 169951232 | bytes 4689924 | tf_op jit(solution)/shard_map/while/body/eval_jaxpr/hqk,khd->qhd/dot_general | solution.py:27
  64.1 0.6 dynamic_slice.31
  66.4 3.5 %fusion.166 = (f32[2,512]{1,0:T(2,128)S(1)}, f32[2,512,1024]{2,1,0:T(8,128)}) fusion(bf16[1024,2,80]{0,2,1:T(8,128)(2,1)S(1)} %get-tuple-element.123, bf16[1024,2,80]{0,2,1:T(8,128)(2,1)S(1)} %get-tuple-element.122, s32[]{:T(128)S(6)} %select_n.43), kind=kOutput, calls=%fused_computation.168.clone.1 | convolution fusion | flops 170918912 | bytes 4689924 | tf_op jit(solution)/shard_map/while/body/eval_jaxpr/sub | solution.py:25
  69.9 3.1 %fusion.167 = bf16[2,512,2,80]{1,3,2,0:T(8,128)(2,1)S(1)} fusion(bf16[2,512,2,80]{1,3,2,0:T(8,128)(2,1)S(1)} %get-tuple-element.111, s32[]{:T(128)S(6)} %copy.31, bf16[1024,2,80]{0,2,1:T(8,128)(2,1)S(1)} %get-tuple-element.124, f32[2,512,1024]{2,1,0:T(8,128)} %get-tuple-element.99, f32[2,512]{1,0:T(2,128)S(1)} %get-tuple-element.100), kind=kOutput, calls=%fused_computation.9.clone.1 | convolution fusion | flops 169951232 | bytes 4689924 | tf_op jit(solution)/shard_map/while/body/eval_jaxpr/hqk,khd->qhd/dot_general | solution.py:27
  73.0 0.3 copy.20
  73.3 0.2 reshape_reshape.3
  73.5 0.8 copy.21
  74.3 3.4 %all-to-all-start.1 = ((bf16[8,128,1,160]{1,3,2,0:T(8,128)(2,1)}), bf16[8,128,1,160]{1,3,2,0:T(8,128)(2,1)S(1)}, u32[]{:S(2)}, u32[]{:S(2)}) async-start(bf16[8,128,1,160]{1,3,2,0:T(8,128)(2,1)} %copy.21), calls=%async_computation.1 | async-start | bytes 655360 | tf_op jit(solution)/shard_map/all_to_all | solution.py:60
  77.9 0.2 reduce_window_sum.11
  78.0 0.2 select_reduce_fusion
  78.3 12.9 %all-to-all-done.1 = bf16[8,128,1,160]{1,3,2,0:T(8,128)(2,1)S(1)} async-done(((bf16[8,128,1,160]{1,3,2,0:T(8,128)(2,1)}), bf16[8,128,1,160]{1,3,2,0:T(8,128)(2,1)S(1)}, u32[]{:S(2)}, u32[]{:S(2)}) %all-to-all-start.1) | async-done | bytes 327712 | tf_op jit(solution)/shard_map/all_to_all | solution.py:60
  91.2 2.7 fusion.145
  93.9 0.2 multiply_reduce_fusion.1
  94.1 0.2 add_convert_fusion
  94.3 0.3 convolution_convert_fusion.3
  94.7 15.1 %all_to_all.53 = bf16[8,12,1280]{2,1,0:T(8,128)(2,1)S(1)} all-to-all(bf16[8,12,1280]{2,1,0:T(8,128)(2,1)S(1)} %reshape.112), channel_id=1, replica_groups=mesh['seq'=8,'exp'=8,'img'=4] {'exp'}, dimensions={0} | all-to-all | bytes 491520 | tf_op jit(solution)/shard_map/all_to_all | solution.py:87
  109.8 0.8 copy.22
  110.6 0.3 convolution_convert_fusion.2
  111.0 11.7 %all_to_all.54 = bf16[8,12,1280]{2,1,0:T(8,128)(2,1)S(1)} all-to-all(bf16[8,12,1280]{2,1,0:T(8,128)(2,1)S(1)} %reshape.116), channel_id=1, replica_groups=mesh['seq'=8,'exp'=8,'img'=4] {'exp'}, dimensions={0} | all-to-all | bytes 491520 | tf_op jit(solution)/shard_map/all_to_all | solution.py:87
  122.7 0.8 copy.24
  123.5 0.2 reduce-scatter.3.cloned.1.call-start
  123.8 20.7 %all-gather.6.cloned.1.call-done = bf16[64,12,1280]{2,0,1:T(8,128)(2,1)} async-done(((bf16[8,12,1280]{2,0,1:T(8,128)(2,1)}), bf16[64,12,1280]{2,0,1:T(8,128)(2,1)}) %all-gather.6.cloned.1.call-update) | async-done | bytes 1966096 | tf_op jit(solution)/shard_map/all_gather | solution.py:94
  144.4 2.6 copy.23
  147.1 2.0 reshape.113
  149.1 9.4 %convolution_convert_fusion.1 = bf16[768,1280]{1,0:T(8,128)(2,1)S(1)} fusion(bf16[2,640,1280]{2,1,0:T(8,128)(2,1)} %param.17, bf16[768,1280]{1,0:T(8,128)(2,1)} %reshape.113, bf16[2,1280,640]{2,1,0:T(8,128)(2,1)} %param.16), kind=kOutput, calls=%fused_computation.18 | convolution fusion | flops 2549514240 | bytes 7208960 | tf_op jit(solution)/shard_map/dot_general | solution.py:99
  158.5 2.2 reshape.114
  160.7 0.3 reduce-scatter.5.cloned.1.call-start
  161.0 24.6 %all-gather.8.cloned.1.call-done = bf16[64,12,1280]{2,0,1:T(8,128)(2,1)} async-done(((bf16[8,12,1280]{2,0,1:T(8,128)(2,1)}), bf16[64,12,1280]{2,0,1:T(8,128)(2,1)}) %all-gather.8.cloned.1.call-update) | async-done | bytes 1966096 | tf_op jit(solution)/shard_map/all_gather | solution.py:94
  185.6 2.6 copy.25
  188.2 2.0 reshape.117
  190.2 9.4 %convolution_convert_fusion = bf16[768,1280]{1,0:T(8,128)(2,1)S(1)} fusion(bf16[2,640,1280]{2,1,0:T(8,128)(2,1)} %param.17, bf16[768,1280]{1,0:T(8,128)(2,1)} %reshape.117, bf16[2,1280,640]{2,1,0:T(8,128)(2,1)} %param.16), kind=kOutput, calls=%fused_computation.17 | convolution fusion | flops 2549514240 | bytes 7208960 | tf_op jit(solution)/shard_map/dot_general | solution.py:99
  199.6 2.1 reshape.118
  201.8 29.1 %reduce-scatter.3.cloned.1.call-done = bf16[8,12,1280]{2,1,0:T(8,128)(2,1)} async-done(((bf16[64,12,1280]{2,1,0:T(8,128)(2,1)}), bf16[8,12,1280]{2,1,0:T(8,128)(2,1)}) %reduce-scatter.3.cloned.1.call-update) | async-done | bytes 245776 | tf_op jit(solution)/shard_map/reduce_scatter | solution.py:102
  230.9 5.8 %all-to-all-start.3 = ((bf16[8,12,1280]{2,1,0:T(8,128)(2,1)}), bf16[8,12,1280]{2,1,0:T(8,128)(2,1)S(1)}, u32[]{:S(2)}, u32[]{:S(2)}) async-start(bf16[8,12,1280]{2,1,0:T(8,128)(2,1)} %reduce-scatter.3.cloned.1.call-done), calls=%async_computation.4 | async-start | bytes 655360 | tf_op jit(solution)/shard_map/all_to_all | solution.py:105
  236.7 40.2 %reduce-scatter.5.cloned.1.call-done = bf16[8,12,1280]{2,1,0:T(8,128)(2,1)} async-done(((bf16[64,12,1280]{2,1,0:T(8,128)(2,1)}), bf16[8,12,1280]{2,1,0:T(8,128)(2,1)}) %reduce-scatter.5.cloned.1.call-update) | async-done | bytes 245776 | tf_op jit(solution)/shard_map/reduce_scatter | solution.py:102
  276.9 5.8 %all-to-all-start.5 = ((bf16[8,12,1280]{2,1,0:T(8,128)(2,1)}), bf16[8,12,1280]{2,1,0:T(8,128)(2,1)S(1)}, u32[]{:S(2)}, u32[]{:S(2)}) async-start(bf16[8,12,1280]{2,1,0:T(8,128)(2,1)} %reduce-scatter.5.cloned.1.call-done), calls=%async_computation.7 | async-start | bytes 655360 | tf_op jit(solution)/shard_map/all_to_all | solution.py:105
  282.8 0.3 convolution_add_fusion.2
  283.1 8.3 %all-to-all-done.5 = bf16[8,12,1280]{2,1,0:T(8,128)(2,1)S(1)} async-done(((bf16[8,12,1280]{2,1,0:T(8,128)(2,1)}), bf16[8,12,1280]{2,1,0:T(8,128)(2,1)S(1)}, u32[]{:S(2)}, u32[]{:S(2)}) %all-to-all-start.5) | async-done | bytes 245792 | tf_op jit(solution)/shard_map/all_to_all | solution.py:105
  291.5 1.0 fusion.26
  (28 shorter events, 0.8 us)
Async XLA Ops:
  6.5 84.7 %all-gather.4.cloned.1.call-start = ((), (), s32[]{:S(2)}) async-start(), calls=%async_computation.8 | async-start | bytes 3686400 | tf_op jit(solution)/shard_map/all_gather | solution.py:65
  9.9 45.2 %all-to-all-start = ((bf16[128,3,8,2,80]{0,4,3,1,2:T(8,128)(2,1)}), bf16[128,3,8,2,80]{0,4,3,1,2:T(8,128)(2,1)S(1)}, u32[]{:S(2)}, u32[]{:S(2)}) async-start(bf16[128,3,8,2,80]{0,4,3,1,2:T(8,128)(2,1)} %copy.18), calls=%async_computation | async-start | bytes 1966080 | tf_op jit(solution)/shard_map/all_to_all | solution.py:58
  73.0 18.2 %copy-start = (bf16[1,128,1280]{2,1,0:T(8,128)(2,1)S(1)}, bf16[1,128,1280]{2,1,0:T(8,128)(2,1)}, u32[]{:S(2)}) copy-start(bf16[1,128,1280]{2,1,0:T(8,128)(2,1)} %param.11) | copy-start | bytes 983044
  74.3 16.9 %all-to-all-start.1 = ((bf16[8,128,1,160]{1,3,2,0:T(8,128)(2,1)}), bf16[8,128,1,160]{1,3,2,0:T(8,128)(2,1)S(1)}, u32[]{:S(2)}, u32[]{:S(2)}) async-start(bf16[8,128,1,160]{1,3,2,0:T(8,128)(2,1)} %copy.21), calls=%async_computation.1 | async-start | bytes 655360 | tf_op jit(solution)/shard_map/all_to_all | solution.py:60
  77.7 66.7 %all-gather.6.cloned.1.call-start = ((), (), s32[]{:S(2)}) async-start(), calls=%async_computation.9 | async-start | bytes 2211840 | tf_op jit(solution)/shard_map/all_gather | solution.py:94
  91.2 2.9 copy-start.1
  91.2 2.9 copy-start.2
  110.6 75.0 %all-gather.8.cloned.1.call-start = ((), (), s32[]{:S(2)}) async-start(), calls=%async_computation.11 | async-start | bytes 2211840 | tf_op jit(solution)/shard_map/all_gather | solution.py:94
  123.5 107.4 %reduce-scatter.3.cloned.1.call-start = ((), (), s32[]{:S(2)}) async-start(), calls=%async_computation.10 | async-start | bytes 2949120 | tf_op jit(solution)/shard_map/reduce_scatter | solution.py:102
  160.7 116.2 %reduce-scatter.5.cloned.1.call-start = ((), (), s32[]{:S(2)}) async-start(), calls=%async_computation.12 | async-start | bytes 2949120 | tf_op jit(solution)/shard_map/reduce_scatter | solution.py:102
  230.9 46.0 %all-to-all-start.3 = ((bf16[8,12,1280]{2,1,0:T(8,128)(2,1)}), bf16[8,12,1280]{2,1,0:T(8,128)(2,1)S(1)}, u32[]{:S(2)}, u32[]{:S(2)}) async-start(bf16[8,12,1280]{2,1,0:T(8,128)(2,1)} %reduce-scatter.3.cloned.1.call-done), calls=%async_computation.4 | async-start | bytes 655360 | tf_op jit(solution)/shard_map/all_to_all | solution.py:105
  276.9 14.5 %all-to-all-start.5 = ((bf16[8,12,1280]{2,1,0:T(8,128)(2,1)}), bf16[8,12,1280]{2,1,0:T(8,128)(2,1)S(1)}, u32[]{:S(2)}, u32[]{:S(2)}) async-start(bf16[8,12,1280]{2,1,0:T(8,128)(2,1)} %reduce-scatter.5.cloned.1.call-done), calls=%async_computation.7 | async-start | bytes 655360 | tf_op jit(solution)/shard_map/all_to_all | solution.py:105
Sparse Core Ops, SparseCore 0:
  9.1 65.1 all-gather.3
  110.7 33.6 all-gather.5
  146.2 39.3 all-gather.7
  188.0 42.8 reduce-scatter.2
  233.3 43.5 reduce-scatter.4

commit v3 on v1

--- a/solution.py
+++ b/solution.py
@@ -60,11 +60,23 @@
     token_heads = lax.all_to_all(attended, "seq", split_axis=0, concat_axis=2, tiled=True).reshape(
         tok_rows, model_width
     )
-    projected_sum = jnp.dot(
-        token_heads,
-        lax.all_gather(attn_proj, "seq", axis=0, tiled=True),
-        preferred_element_type=jnp.float32,
+    img_count = lax.axis_size("img")
+    core = lax.axis_index("img") % 2
+    half_width = model_width // 2
+    proj_half = lax.all_gather(
+        lax.dynamic_slice_in_dim(attn_proj, core * half_width, half_width, axis=1),
+        "seq",
+        axis=0,
+        tiled=True,
     )
+    sibling = [(i, i ^ 1) for i in range(img_count)]
+    proj_other = lax.ppermute(proj_half, "img", sibling)
+    proj_full = jnp.zeros((model_width, model_width), jnp.bfloat16)
+    proj_full = lax.dynamic_update_slice_in_dim(proj_full, proj_half, core * half_width, axis=1)
+    proj_full = lax.dynamic_update_slice_in_dim(
+        proj_full, proj_other, (1 - core) * half_width, axis=1
+    )
+    projected_sum = jnp.dot(token_heads, proj_full, preferred_element_type=jnp.float32)
     stream_own = residual[0].astype(jnp.float32) + projected_sum
     stream = stream_own.astype(jnp.bfloat16)
     stream_own = stream.astype(jnp.float32)

time: 291 us -> 297 us (1.021)
  local copies, waits for them, and re-layouts: 34.1 us -> 43.2 us
  waiting for transfers between devices: 147 us -> 144 us
    dynamic_update_slice x0 -> x2, local copies, waits for them, and re-layouts: none -> 5.65 us  [the longest x1 2.83 us: per_device(): lax.dynamic_update_slice_in_dim(proj_full, proj_other, (1 - core) * half_...]
    all_to_all x1, waiting for transfers between devices: 11.7 us -> 6.62 us  [per_device(): lax.all_to_all(attended, 'seq', split_axis=0, concat_axis=2, tiled=True)]
    all_gather x1, waiting for transfers between devices: 0.01 us -> 3.66 us  [per_device(): lax.all_gather(lax.dynamic_slice_in_dim(attn_proj, core * half_width, hal...]
  transfers between devices with their start and end apart: 5 -> 6, of which waited for: 4 -> 5; matrix products, arithmetic and copies ran while one was open for 11% -> 13% of each run, Pallas kernels for 0% -> 0%
where the time goes in v3:
time: 297 us; the launch traced here: 296 us
  waiting for transfers between devices  144 us (48%)
  matrix products  44.9 us (15%)
  local copies, waits for them, and re-layouts  43.2 us (15%)
  blocking collectives  33.4 us (11%)
  between operations  13.2 us (4%)
  starting transfers between devices  12.8 us (4%)
  loops' own time  3.82 us (1%)
    reduce_scatter x1, waiting for transfers between devices, per_device(): summed = lax.psum_scatter(pieces, 'seq', scatter_dimension=0, tiled=True)[0]  51.6 us
    all_gather x1, waiting for transfers between devices, per_device(): gathered = lax.all_gather(arrived, 'seq', axis=0, tiled=False)  45.6 us
    all_to_all x1, waiting for transfers between devices, per_device(): lax.all_to_all(regrouped, 'seq', split_axis=2, concat_axis=0, tiled=True)  36.2 us
    dot_general x1, matrix products, per_device(): jnp.einsum('sejcf,jfd->sejcd', hidden, expert_down, preferred_element_typ...  22.1 us
    all_to_all x1, blocking collectives, per_device(): lax.all_to_all(dispatch, 'exp', split_axis=0, concat_axis=0, tiled=True)  16.9 us
    all_to_all x1, blocking collectives, per_device(): lax.all_to_all(summed, 'exp', split_axis=0, concat_axis=0, tiled=True)  16.5 us
    sub x2, matrix products, one_block(): powers = jnp.exp(scores - peak)  9.09 us
    all_to_all x1, starting transfers between devices, per_device(): lax.all_to_all(regrouped, 'seq', split_axis=2, concat_axis=0, tiled=True)  8.47 us
  transfers between devices with their start and end apart: 6, of which 5 were waited for; matrix products, arithmetic and copies ran while one was open for 13% of the time, Pallas kernels for 0%

profile of v3, /device:TPU:8, one launch (start us, length us, event | category | flops | bytes accessed | tf_op | source)
XLA Modules:
  0.0 296.3 jit_solution(8026337228120255540)
XLA Ops:
  6.5 1.8 constant_dynamic-slice_fusion.1
  8.3 2.2 copy.22
  10.6 2.2 copy.23
  12.8 8.5 %all-to-all-start = ((bf16[128,3,8,2,80]{0,4,3,1,2:T(8,128)(2,1)}), bf16[128,3,8,2,80]{0,4,3,1,2:T(8,128)(2,1)}, u32[]{:S(2)}, u32[]{:S(2)}) async-start(bf16[128,3,8,2,80]{0,4,3,1,2:T(8,128)(2,1)} %copy.23), calls=%async_computation | async-start | bytes 1966080 | tf_op jit(solution)/shard_map/all_to_all | solution.py:58
  21.3 0.7 fusion.69
  21.9 0.1 fusion.68
  22.0 0.2 reduce_window_sum.11
  22.2 0.2 select_reduce_fusion
  22.4 0.7 multiply_add_fusion
  23.0 36.2 %all-to-all-done = bf16[128,3,8,2,80]{0,4,3,1,2:T(8,128)(2,1)} async-done(((bf16[128,3,8,2,80]{0,4,3,1,2:T(8,128)(2,1)}), bf16[128,3,8,2,80]{0,4,3,1,2:T(8,128)(2,1)}, u32[]{:S(2)}, u32[]{:S(2)}) %all-to-all-start) | async-done | bytes 983072 | tf_op jit(solution)/shard_map/all_to_all | solution.py:58
  59.2 1.3 copy_bitcast_fusion
  60.5 1.0 slice_bitcast_fusion
  61.6 3.7 %all-gather.4.cloned.1.call-done = bf16[1280,640]{1,0:T(8,128)(2,1)} async-done(((bf16[160,640]{1,0:T(8,128)(2,1)}), bf16[1280,640]{1,0:T(8,128)(2,1)}) %all-gather.4.cloned.1.call-update) | async-done | bytes 1638416 | tf_op jit(solution)/shard_map/all_gather | solution.py:66
  65.2 21.6 %while.10 = (s32[]{:T(128)}, bf16[2,512,2,80]{1,3,2,0:T(8,128)(2,1)}, s32[2]{0:T(128)S(1)}, bf16[1024,2,80]{0,2,1:T(8,128)(2,1)}, bf16[1024,2,80]{0,2,1:T(8,128)...) while((s32[]{:T(128)}, bf16[2,512,2,80]{1,3,2,0:T(8,128)(2,1)}, ...), condition=%wide.region_3.4_spmd, body=%wide.region_0.3_spmd.sunk | while | flops 340870144 | bytes 9379995 | solution.py:31
  65.2 0.6 dynamic_slice.39
  67.7 4.6 %fusion.122 = (f32[2,512]{1,0:T(2,128)S(1)}, f32[2,512,1024]{2,1,0:T(8,128)}) fusion(bf16[1024,2,80]{0,2,1:T(8,128)(2,1)} %get-tuple-element.120, bf16[1024,2,80]{0,2,1:T(8,128)(2,1)} %get-tuple-element.119, s32[]{:T(128)S(6)} %select_n.25), kind=kOutput, calls=%fused_computation.119.clone.1 | convolution fusion | flops 170918912 | bytes 4689924 | tf_op jit(solution)/shard_map/while/body/eval_jaxpr/sub | solution.py:25
  72.3 3.7 %fusion.123 = bf16[2,512,2,80]{1,3,2,0:T(8,128)(2,1)} fusion(bf16[2,512,2,80]{1,3,2,0:T(8,128)(2,1)} %get-tuple-element.108, s32[]{:T(128)S(6)} %copy.39, bf16[1024,2,80]{0,2,1:T(8,128)(2,1)} %get-tuple-element.121, f32[2,512,1024]{2,1,0:T(8,128)} %get-tuple-element.96, f32[2,512]{1,0:T(2,128)S(1)} %get-tuple-element.97), kind=kOutput, calls=%fused_computation.9.clone.1 | convolution fusion | flops 169951232 | bytes 4689924 | tf_op jit(solution)/shard_map/while/body/eval_jaxpr/hqk,khd->qhd/dot_general | solution.py:27
  76.0 0.6 dynamic_slice.39
  78.6 4.5 %fusion.122 = (f32[2,512]{1,0:T(2,128)S(1)}, f32[2,512,1024]{2,1,0:T(8,128)}) fusion(bf16[1024,2,80]{0,2,1:T(8,128)(2,1)} %get-tuple-element.120, bf16[1024,2,80]{0,2,1:T(8,128)(2,1)} %get-tuple-element.119, s32[]{:T(128)S(6)} %select_n.25), kind=kOutput, calls=%fused_computation.119.clone.1 | convolution fusion | flops 170918912 | bytes 4689924 | tf_op jit(solution)/shard_map/while/body/eval_jaxpr/sub | solution.py:25
  83.1 3.7 %fusion.123 = bf16[2,512,2,80]{1,3,2,0:T(8,128)(2,1)} fusion(bf16[2,512,2,80]{1,3,2,0:T(8,128)(2,1)} %get-tuple-element.108, s32[]{:T(128)S(6)} %copy.39, bf16[1024,2,80]{0,2,1:T(8,128)(2,1)} %get-tuple-element.121, f32[2,512,1024]{2,1,0:T(8,128)} %get-tuple-element.96, f32[2,512]{1,0:T(2,128)S(1)} %get-tuple-element.97), kind=kOutput, calls=%fused_computation.9.clone.1 | convolution fusion | flops 169951232 | bytes 4689924 | tf_op jit(solution)/shard_map/while/body/eval_jaxpr/hqk,khd->qhd/dot_general | solution.py:27
  86.8 2.0 copy.25
  88.9 1.9 reshape_reshape.3
  90.8 1.7 copy.26
  92.5 4.1 %all-to-all-start.1 = ((bf16[8,128,1,160]{1,3,2,0:T(8,128)(2,1)}), bf16[8,128,1,160]{1,3,2,0:T(8,128)(2,1)}, u32[]{:S(2)}, u32[]{:S(2)}) async-start(bf16[8,128,1,160]{1,3,2,0:T(8,128)(2,1)} %copy.26), calls=%async_computation.1 | async-start | bytes 655360 | tf_op jit(solution)/shard_map/all_to_all | solution.py:60
  96.6 0.0 all-gather.6.cloned.1.call-start
  96.6 1.9 broadcast_in_dim.13
  98.5 2.8 constant_dynamic-update-slice_fusion.1
  101.3 2.8 constant_dynamic-update-slice_fusion
  104.2 6.6 %all-to-all-done.1 = bf16[8,128,1,160]{1,3,2,0:T(8,128)(2,1)} async-done(((bf16[8,128,1,160]{1,3,2,0:T(8,128)(2,1)}), bf16[8,128,1,160]{1,3,2,0:T(8,128)(2,1)}, u32[]{:S(2)}, u32[]{:S(2)}) %all-to-all-start.1) | async-done | bytes 327712 | tf_op jit(solution)/shard_map/all_to_all | solution.py:60
  110.8 2.8 fusion.105
  113.6 0.2 multiply_reduce_fusion.1
  113.8 0.6 copy-done.1
  114.4 1.2 convolution_convert_fusion.1
  115.6 2.0 reshape.40
  117.6 1.5 copy.27
  119.1 16.9 %all_to_all.43 = bf16[8,2,12,1280]{3,1,2,0:T(2,128)(2,1)} all-to-all(bf16[8,2,12,1280]{3,1,2,0:T(2,128)(2,1)S(1)} %copy.27), channel_id=1, replica_groups=mesh['seq'=8,'exp'=8,'img'=4] {'exp'}, dimensions={0} | all-to-all | bytes 983040 | tf_op jit(solution)/shard_map/all_to_all | solution.py:97
  136.0 0.0 all-gather.6.cloned.1.call-update
  136.0 0.2 reduce-scatter.2.cloned.1.call-start
  136.3 45.6 %all-gather.6.cloned.1.call-done = bf16[64,2,12,1280]{3,1,2,0:T(2,128)(2,1)} async-done(((bf16[8,2,12,1280]{3,1,2,0:T(2,128)(2,1)}), bf16[64,2,12,1280]{3,1,2,0:T(2,128)(2,1)}) %all-gather.6.cloned.1.call-update) | async-done | bytes 3932176 | tf_op jit(solution)/shard_map/all_gather | solution.py:98
  181.9 5.2 %copy.28 = bf16[64,2,12,1280]{3,2,0,1:T(8,128)(2,1)} copy(bf16[64,2,12,1280]{3,1,2,0:T(2,128)(2,1)} %all-gather.6.cloned.1.call-done) | data formatting | bytes 7864320 | tf_op jit(solution)/shard_map/all_gather | solution.py:98
  187.0 22.1 %fusion.41 = bf16[8,8,2,12,1280]{4,3,1,0,2:T(8,128)(2,1)} fusion(bf16[2,640,1280]{2,1,0:T(8,128)(2,1)S(1)} %copy-done, bf16[8,8,2,12,1280]{4,3,1,0,2:T(8,128)(2,1)} %bitcast.136, bf16[2,1280,640]{2,1,0:T(8,128)(2,1)} %param.16), kind=kOutput, calls=%fused_computation.42 | convolution fusion | flops 5099028480 | bytes 14417920 | tf_op jit(solution)/shard_map/sejcf,jfd->sejcd/dot_general | solution.py:103
  209.1 5.9 %copy.29 = bf16[8,8,2,12,1280]{4,1,3,2,0:T(8,128)(2,1)} copy(bf16[8,8,2,12,1280]{4,3,1,0,2:T(8,128)(2,1)} %fusion.41) | data formatting | bytes 7864320 | tf_op jit(solution)/shard_map/convert_element_type | solution.py:105
  215.0 51.6 %reduce-scatter.2.cloned.1.call-done = bf16[1,8,2,12,1280]{4,1,3,2,0:T(8,128)(2,1)} async-done(((bf16[8,8,2,12,1280]{4,1,3,2,0:T(8,128)(2,1)}), bf16[1,8,2,12,1280]{4,1,3,2,0:T(8,128)(2,1)}) %reduce-scatter.2.cloned.1.call-update) | async-done | bytes 491536 | tf_op jit(solution)/shard_map/reduce_scatter | solution.py:106
  266.6 1.5 copy.30
  268.2 16.5 %all_to_all.44 = bf16[8,2,12,1280]{3,1,2,0:T(2,128)(2,1)S(1)} all-to-all(bf16[8,2,12,1280]{3,1,2,0:T(2,128)(2,1)S(1)} %copy.30), channel_id=1, replica_groups=mesh['seq'=8,'exp'=8,'img'=4] {'exp'}, dimensions={0} | all-to-all | bytes 983040 | tf_op jit(solution)/shard_map/all_to_all | solution.py:107
  284.7 0.9 copy.31
  285.6 2.0 reshape.41
  287.5 2.3 fusion.65
  (16 shorter events, 0.1 us)
Async XLA Ops:
  6.5 180.5 %copy-start = (bf16[2,640,1280]{2,1,0:T(8,128)(2,1)S(1)}, bf16[2,640,1280]{2,1,0:T(8,128)(2,1)}, u32[]{:S(2)}) copy-start(bf16[2,640,1280]{2,1,0:T(8,128)(2,1)} %param.17) | copy-start | bytes 9830404
  6.5 58.7 %all-gather.4.cloned.1.call-start = ((), (), s32[]{:S(2)}) async-start(), calls=%async_computation.5 | async-start | bytes 1843200 | tf_op jit(solution)/shard_map/all_gather | solution.py:66
  12.8 46.4 %all-to-all-start = ((bf16[128,3,8,2,80]{0,4,3,1,2:T(8,128)(2,1)}), bf16[128,3,8,2,80]{0,4,3,1,2:T(8,128)(2,1)}, u32[]{:S(2)}, u32[]{:S(2)}) async-start(bf16[128,3,8,2,80]{0,4,3,1,2:T(8,128)(2,1)} %copy.23), calls=%async_computation | async-start | bytes 1966080 | tf_op jit(solution)/shard_map/all_to_all | solution.py:58
  65.2 36.1 %collective-permute-start = (bf16[1280,640]{1,0:T(8,128)(2,1)}, bf16[1280,640]{1,0:T(8,128)(2,1)}, u32[]{:S(2)}, u32[]{:S(2)}) collective-permute-start(bf16[1280,640]{1,0:T(8,128)(2,1)} %all-gather.4.cloned.1.call-done), channel_id=1, source_target_pairs={{0,1},{1,0},{2,3},{3,2},{4,5},{5,4},{6,7},{7,6},{8,9},{9,8},{10,11... | collective-permute-start | bytes 4915208 | tf_op jit(solution)/shard_map/ppermute | solution.py:73
  92.5 18.3 %all-to-all-start.1 = ((bf16[8,128,1,160]{1,3,2,0:T(8,128)(2,1)}), bf16[8,128,1,160]{1,3,2,0:T(8,128)(2,1)}, u32[]{:S(2)}, u32[]{:S(2)}) async-start(bf16[8,128,1,160]{1,3,2,0:T(8,128)(2,1)} %copy.26), calls=%async_computation.1 | async-start | bytes 655360 | tf_op jit(solution)/shard_map/all_to_all | solution.py:60
  96.6 85.3 %all-gather.6.cloned.1.call-start = ((), (), s32[]{:S(2)}) async-start(), calls=%async_computation.7 | async-start | bytes 4423680 | tf_op jit(solution)/shard_map/all_gather | solution.py:98
  98.5 15.9 %copy-start.2 = (f32[1280]{0:T(1024)S(1)}, f32[1280]{0:T(1024)}, u32[]{:S(2)}) copy-start(f32[1280]{0:T(1024)} %param.14) | copy-start | bytes 15364
  98.5 15.9 %copy-start.3 = (f32[1280]{0:T(1024)S(1)}, f32[1280]{0:T(1024)}, u32[]{:S(2)}) copy-start(f32[1280]{0:T(1024)} %param.13) | copy-start | bytes 15364
  113.6 0.9 copy-start.1
  136.0 130.6 %reduce-scatter.2.cloned.1.call-start = ((), (), s32[]{:S(2)}) async-start(), calls=%async_computation.6 | async-start | bytes 4423680 | tf_op jit(solution)/shard_map/reduce_scatter | solution.py:106
Sparse Core Ops, SparseCore 0:
  9.1 56.0 all-gather.3
  136.2 45.6 all-gather.5
  215.2 51.4 reduce-scatter.1
